TPU v7x, 512 devices: a whole 4x8x8 slice. The times are simulated.
512 devices in a mesh: group: 8 (over x, y_hi), sub: 64 (over y_lo, z, core).
Axes of the slice: x: 4, y: 8 (y_hi: 2, y_lo: 4; y = y_hi * 4 + y_lo), z: 8, core: 2. Of those that a mesh axis runs over, the one named last changes fastest.
Arguments:
- modes: bfloat16 [524288, 512], P(('group', 'sub')), may hold values from -6 to 6
- block_vals: bfloat16 [24576, 128, 128], P(('group', 'sub')), may hold values from -0.21875 to 0.21875
- block_cols: int32 [24576], P(('group', 'sub')), may hold values from 0 to 7, as said below
- level_maps: bfloat16 [2, 128, 128], replicated, may hold values from -0.5 to 0.5
- psi: bfloat16 [524288, 512], P(('group', 'sub')), may hold values from -0.09375 to 0.09375
- parent_vals: bfloat16 [4096, 128, 128], P(('group', 'sub')), may hold values from -0.09375 to 0.09375
- parent_rows: int32 [4096], P(('group', 'sub')), may hold values from 0 to 63
Outputs:
- parent_coupling: bfloat16 [8192, 1024], P('sub', 'group')
- projected: float32 [4096, 512], P(('group', 'sub'))
Inputs may be any that keep to these rules, and one draw needn't show every extreme that they name: `block_cols`: within one interface row block of one device the 6 vertex blocks are distinct.
All inputs are finite; a program needn't handle non-finite values.
Results may differ from a plain program's by a relative error of at most 0.0078.
Values may be sent and summed in bfloat16 or wider, within the bound.
No kernel may reach another device: no remote copies, remote signals or barrier semaphores. Data moves between devices by JAX's collectives and lax.ppermute only.
A program may use at most 64 MiB of HBM per device.

v0:
```python
import jax
import jax.numpy as jnp
from jax import lax
from jax.sharding import PartitionSpec as P

IFB = 8
BPR = 6


def from_partner(value, axis, mask):
    pairs = [(source, source ^ mask) for source in range(lax.axis_size(axis))]
    return lax.ppermute(value, axis, pairs)


def on_device(modes, block_vals, block_cols, level_maps, psi, parent_vals, parent_rows):
    block_size = block_vals.shape[1]
    width = modes.shape[1]
    vertex_blocks = modes.shape[0] // block_size
    row_blocks = IFB
    levels = min(2, lax.axis_size("group").bit_length() - 1)
    merged = 2**levels
    n_sub = lax.axis_size("sub")
    group_index = lax.axis_index("group")
    vals_all = [parent_vals]
    rows_all = [parent_rows]
    for mask in range(1, merged):
        vals_all.append(from_partner(parent_vals, "group", mask))
        rows_all.append(from_partner(parent_rows, "group", mask))
    vals_all = jnp.concatenate(vals_all, axis=0)
    rows_all = jnp.concatenate(rows_all, axis=0)
    onehot = (
        block_cols.reshape(row_blocks, BPR)[:, :, None] == jnp.arange(vertex_blocks)[None, None, :]
    ).astype(jnp.float32)
    blocks = block_vals.astype(jnp.float32).reshape(row_blocks, BPR, block_size, block_size)
    dense = (
        jnp.einsum("rbc,rbij->ricj", onehot, blocks)
        .reshape(row_blocks * block_size, vertex_blocks * block_size)
        .astype(jnp.bfloat16)
    )
    panel = jnp.dot(dense, modes, preferred_element_type=jnp.float32).astype(jnp.bfloat16)
    for level in range(levels):
        sibling = from_partner(panel, "group", 2**level)
        total = (panel.astype(jnp.float32) + sibling.astype(jnp.float32)).astype(jnp.bfloat16)
        mapped = jnp.einsum(
            "ab,rbm->ram",
            level_maps[level],
            total.reshape(row_blocks, block_size, width),
            preferred_element_type=jnp.float32,
        )
        panel = mapped.reshape(row_blocks * block_size, width).astype(jnp.bfloat16)
    quarter = width // merged
    column = group_index % merged * quarter
    head = lax.dynamic_slice_in_dim(panel[:block_size], column, quarter, 1)
    piece = lax.all_gather(head, "sub", axis=0, tiled=True).reshape(n_sub, block_size, quarter)
    picked = jnp.take(piece, rows_all, axis=0)
    parent_out = jnp.einsum(
        "kab,kbm->am", vals_all, picked, preferred_element_type=jnp.float32
    ).astype(jnp.bfloat16)
    partial = lax.dot_general(
        psi, panel, (((0,), (0,)), ((), ())), preferred_element_type=jnp.float32
    )
    spread = lax.all_to_all(partial.reshape(n_sub, width // n_sub, width), "sub", 0, 0, tiled=True)
    projected = spread.sum(axis=0)
    return (parent_out, projected)


def solution(mesh):
    return jax.shard_map(
        on_device,
        mesh=mesh,
        in_specs=(
            P(("group", "sub"), None),
            P(("group", "sub"), None, None),
            P(("group", "sub")),
            P(),
            P(("group", "sub"), None),
            P(("group", "sub"), None, None),
            P(("group", "sub")),
        ),
        out_specs=(P("sub", "group"), P(("group", "sub"), None)),
        check_vma=False,
    )
```

profile of v0, /device:TPU:1, one launch (start us, length us, event | category | flops | bytes accessed | tf_op | source)
XLA Modules:
  0.0 253.6 jit_solution(811477235119022073)
XLA Ops:
  7.2 0.8 eq.17
  8.1 0.5 copy-done
  8.6 1.0 fusion.5
  9.8 1.2 fusion.8
  11.1 8.4 %collective-permute-start.6 = (bf16[1024,512]{1,0:T(8,128)(2,1)S(1)}, bf16[1024,512]{1,0:T(8,128)(2,1)S(1)}, u32[]{:S(2)}, u32[]{:S(2)}) collective-permute-start(bf16[1024,512]{1,0:T(8,128)(2,1)S(1)} %fusion.8), channel_id=1, source_target_pairs={{0,64},{64,0},{128,192},{192,128},{256,320},{320,256},{384,448},{4... | collective-permute-start | bytes 3145736 | tf_op jit(solution)/shard_map/ppermute | solution.py:12
  19.5 33.9 %collective-permute-done.6 = bf16[1024,512]{1,0:T(8,128)(2,1)S(1)} collective-permute-done((bf16[1024,512]{1,0:T(8,128)(2,1)S(1)}, bf16[1024,512]{1,0:T(8,128)(2,1)S(1)}, u32[]{:S(2)}, u32[]{:S(2)}) %collective-permute-start.6) | collective-permute-done | bytes 1048608 | tf_op jit(solution)/shard_map/ppermute | solution.py:12
  54.2 3.7 %collective-permute-start.7 = (bf16[1024,512]{1,0:T(8,128)(2,1)S(1)}, bf16[1024,512]{1,0:T(8,128)(2,1)}, u32[]{:S(2)}, u32[]{:S(2)}) collective-permute-start(bf16[1024,512]{1,0:T(8,128)(2,1)S(1)} %bitcast.52), channel_id=1, source_target_pairs={{0,128},{64,192},{128,0},{192,64},{256,384},{320,448},{384,256},{4... | collective-permute-start | bytes 3145736 | tf_op jit(solution)/shard_map/ppermute | solution.py:12
  57.9 12.3 %collective-permute-done.7 = bf16[1024,512]{1,0:T(8,128)(2,1)} collective-permute-done((bf16[1024,512]{1,0:T(8,128)(2,1)S(1)}, bf16[1024,512]{1,0:T(8,128)(2,1)}, u32[]{:S(2)}, u32[]{:S(2)}) %collective-permute-start.7) | collective-permute-done | bytes 1048608 | tf_op jit(solution)/shard_map/ppermute | solution.py:12
  70.1 1.5 add_convert_fusion
  72.1 0.6 constant_dynamic-slice_fusion
  72.7 3.0 %convolution_bitcast_fusion = f32[64,8,512]{2,1,0:T(8,128)} fusion(bf16[1024,512]{1,0:T(8,128)(2,1)S(1)} %bitcast.57, bf16[1024,512]{1,0:T(8,128)(2,1)} %param.11), kind=kOutput, calls=%fused_computation.12 | convolution fusion | flops 536870912 | bytes 3145728 | tf_op jit(solution)/shard_map/dot_general | solution.py:59
  75.7 36.6 %all-to-all-start = ((f32[64,8,512]{2,1,0:T(8,128)}), f32[64,8,512]{2,1,0:T(8,128)S(1)}, u32[]{:S(2)}, u32[]{:S(2)}) async-start(f32[64,8,512]{2,1,0:T(8,128)} %convolution_bitcast_fusion), calls=%async_computation | async-start | bytes 2097152 | tf_op jit(solution)/shard_map/all_to_all | solution.py:62
  112.3 4.8 %collective-permute-start.3 = (s32[8]{0:T(128)S(1)}, s32[8]{0:T(128)S(1)}, u32[]{:S(2)}, u32[]{:S(2)}) collective-permute-start(s32[8]{0:T(128)S(1)} %copy-done.2), channel_id=1, source_target_pairs={{0,64},{64,0},{128,192},{192,128},{256,320},{320,256},{384,448},{4... | collective-permute-start | bytes 104 | tf_op jit(solution)/shard_map/ppermute | solution.py:12
  117.2 3.1 %collective-permute-start.4 = (s32[8]{0:T(128)S(1)}, s32[8]{0:T(128)S(1)}, u32[]{:S(2)}, u32[]{:S(2)}) collective-permute-start(s32[8]{0:T(128)S(1)} %copy-done.2), channel_id=1, source_target_pairs={{0,128},{64,192},{128,0},{192,64},{256,384},{320,448},{384,256},{4... | collective-permute-start | bytes 104 | tf_op jit(solution)/shard_map/ppermute | solution.py:12
  120.3 4.3 %collective-permute-start.5 = (s32[8]{0:T(128)S(1)}, s32[8]{0:T(128)S(1)}, u32[]{:S(2)}, u32[]{:S(2)}) collective-permute-start(s32[8]{0:T(128)S(1)} %copy-done.2), channel_id=1, source_target_pairs={{0,192},{64,128},{128,64},{192,0},{256,448},{320,384},{384,320},{4... | collective-permute-start | bytes 104 | tf_op jit(solution)/shard_map/ppermute | solution.py:12
  124.6 4.8 %collective-permute-start = (bf16[8,128,128]{2,1,0:T(8,128)(2,1)S(1)}, bf16[8,128,128]{2,1,0:T(8,128)(2,1)S(1)}, u32[]{:S(2)}, u32[]{:S(2)}) collective-permute-start(bf16[8,128,128]{2,1,0:T(8,128)(2,1)S(1)} %copy-done.4), channel_id=1, source_target_pairs={{0,64},{64,0},{128,192},{192,128},{256,320},{320,256},{384,448},{4... | collective-permute-start | bytes 786440 | tf_op jit(solution)/shard_map/ppermute | solution.py:12
  129.5 3.1 %collective-permute-start.1 = (bf16[8,128,128]{2,1,0:T(8,128)(2,1)S(1)}, bf16[8,128,128]{2,1,0:T(8,128)(2,1)S(1)}, u32[]{:S(2)}, u32[]{:S(2)}) collective-permute-start(bf16[8,128,128]{2,1,0:T(8,128)(2,1)S(1)} %copy-done.4), channel_id=1, source_target_pairs={{0,128},{64,192},{128,0},{192,64},{256,384},{320,448},{384,256},{4... | collective-permute-start | bytes 786440 | tf_op jit(solution)/shard_map/ppermute | solution.py:12
  132.6 0.5 collective-permute-done.3
  133.1 5.8 %collective-permute-start.2 = (bf16[8,128,128]{2,1,0:T(8,128)(2,1)S(1)}, bf16[8,128,128]{2,1,0:T(8,128)(2,1)}, u32[]{:S(2)}, u32[]{:S(2)}) collective-permute-start(bf16[8,128,128]{2,1,0:T(8,128)(2,1)S(1)} %copy-done.4), channel_id=1, source_target_pairs={{0,192},{64,128},{128,64},{192,0},{256,448},{320,384},{384,320},{4... | collective-permute-start | bytes 786440 | tf_op jit(solution)/shard_map/ppermute | solution.py:12
  139.0 25.7 %all-to-all-done = f32[64,8,512]{2,1,0:T(8,128)S(1)} async-done(((f32[64,8,512]{2,1,0:T(8,128)}), f32[64,8,512]{2,1,0:T(8,128)S(1)}, u32[]{:S(2)}, u32[]{:S(2)}) %all-to-all-start) | async-done | bytes 1048608 | tf_op jit(solution)/shard_map/all_to_all | solution.py:62
  164.7 0.7 reduce_sum.9
  165.4 76.8 %all-gather.3.cloned.1.call-done = bf16[1,8192,128]{2,1,0:T(8,128)(2,1)} async-done(((bf16[1,128,128]{2,1,0:T(8,128)(2,1)}), bf16[1,8192,128]{2,1,0:T(8,128)(2,1)}) %all-gather.3.cloned.1.call-update) | async-done | bytes 2097168 | tf_op jit(solution)/shard_map/all_gather | solution.py:54
  242.3 2.3 gather_fusion
  244.7 2.1 fusion.11
  (23 shorter events, 1.6 us)
Async XLA Ops:
  7.2 1.4 copy-start
  7.2 235.1 %all-gather.3.cloned.1.call-start = ((), (), s32[]{:S(2)}) async-start(), calls=%async_computation.1 | async-start | bytes 2129920 | tf_op jit(solution)/shard_map/all_gather | solution.py:54
  8.6 1.2 copy-start.3
  11.1 42.7 %copy-start.1 = (bf16[2,128,128]{2,1,0:T(8,128)(2,1)S(1)}, bf16[2,128,128]{2,1,0:T(8,128)(2,1)}, u32[]{:S(2)}) copy-start(bf16[2,128,128]{2,1,0:T(8,128)(2,1)} %param.10) | copy-start | bytes 196612
  11.1 42.3 %collective-permute-start.6 = (bf16[1024,512]{1,0:T(8,128)(2,1)S(1)}, bf16[1024,512]{1,0:T(8,128)(2,1)S(1)}, u32[]{:S(2)}, u32[]{:S(2)}) collective-permute-start(bf16[1024,512]{1,0:T(8,128)(2,1)S(1)} %fusion.8), channel_id=1, source_target_pairs={{0,64},{64,0},{128,192},{192,128},{256,320},{320,256},{384,448},{4... | collective-permute-start | bytes 3145736 | tf_op jit(solution)/shard_map/ppermute | solution.py:12
  54.2 16.0 %collective-permute-start.7 = (bf16[1024,512]{1,0:T(8,128)(2,1)S(1)}, bf16[1024,512]{1,0:T(8,128)(2,1)}, u32[]{:S(2)}, u32[]{:S(2)}) collective-permute-start(bf16[1024,512]{1,0:T(8,128)(2,1)S(1)} %bitcast.52), channel_id=1, source_target_pairs={{0,128},{64,192},{128,0},{192,64},{256,384},{320,448},{384,256},{4... | collective-permute-start | bytes 3145736 | tf_op jit(solution)/shard_map/ppermute | solution.py:12
  75.7 36.6 %copy-start.2 = (s32[8]{0:T(128)S(1)}, s32[8]{0:T(128)}, u32[]{:S(2)}) copy-start(s32[8]{0:T(128)} %param.13) | copy-start | bytes 100
  75.7 48.9 %copy-start.4 = (bf16[8,128,128]{2,1,0:T(8,128)(2,1)S(1)}, bf16[8,128,128]{2,1,0:T(8,128)(2,1)}, u32[]{:S(2)}) copy-start(bf16[8,128,128]{2,1,0:T(8,128)(2,1)} %param.12) | copy-start | bytes 786436
  75.7 89.0 %all-to-all-start = ((f32[64,8,512]{2,1,0:T(8,128)}), f32[64,8,512]{2,1,0:T(8,128)S(1)}, u32[]{:S(2)}, u32[]{:S(2)}) async-start(f32[64,8,512]{2,1,0:T(8,128)} %convolution_bitcast_fusion), calls=%async_computation | async-start | bytes 2097152 | tf_op jit(solution)/shard_map/all_to_all | solution.py:62
  112.3 20.8 %collective-permute-start.3 = (s32[8]{0:T(128)S(1)}, s32[8]{0:T(128)S(1)}, u32[]{:S(2)}, u32[]{:S(2)}) collective-permute-start(s32[8]{0:T(128)S(1)} %copy-done.2), channel_id=1, source_target_pairs={{0,64},{64,0},{128,192},{192,128},{256,320},{320,256},{384,448},{4... | collective-permute-start | bytes 104 | tf_op jit(solution)/shard_map/ppermute | solution.py:12
  117.2 21.7 %collective-permute-start.4 = (s32[8]{0:T(128)S(1)}, s32[8]{0:T(128)S(1)}, u32[]{:S(2)}, u32[]{:S(2)}) collective-permute-start(s32[8]{0:T(128)S(1)} %copy-done.2), channel_id=1, source_target_pairs={{0,128},{64,192},{128,0},{192,64},{256,384},{320,448},{384,256},{4... | collective-permute-start | bytes 104 | tf_op jit(solution)/shard_map/ppermute | solution.py:12
  120.3 18.6 %collective-permute-start.5 = (s32[8]{0:T(128)S(1)}, s32[8]{0:T(128)S(1)}, u32[]{:S(2)}, u32[]{:S(2)}) collective-permute-start(s32[8]{0:T(128)S(1)} %copy-done.2), channel_id=1, source_target_pairs={{0,192},{64,128},{128,64},{192,0},{256,448},{320,384},{384,320},{4... | collective-permute-start | bytes 104 | tf_op jit(solution)/shard_map/ppermute | solution.py:12
  124.6 120.0 %collective-permute-start = (bf16[8,128,128]{2,1,0:T(8,128)(2,1)S(1)}, bf16[8,128,128]{2,1,0:T(8,128)(2,1)S(1)}, u32[]{:S(2)}, u32[]{:S(2)}) collective-permute-start(bf16[8,128,128]{2,1,0:T(8,128)(2,1)S(1)} %copy-done.4), channel_id=1, source_target_pairs={{0,64},{64,0},{128,192},{192,128},{256,320},{320,256},{384,448},{4... | collective-permute-start | bytes 786440 | tf_op jit(solution)/shard_map/ppermute | solution.py:12
  129.5 115.2 %collective-permute-start.1 = (bf16[8,128,128]{2,1,0:T(8,128)(2,1)S(1)}, bf16[8,128,128]{2,1,0:T(8,128)(2,1)S(1)}, u32[]{:S(2)}, u32[]{:S(2)}) collective-permute-start(bf16[8,128,128]{2,1,0:T(8,128)(2,1)S(1)} %copy-done.4), channel_id=1, source_target_pairs={{0,128},{64,192},{128,0},{192,64},{256,384},{320,448},{384,256},{4... | collective-permute-start | bytes 786440 | tf_op jit(solution)/shard_map/ppermute | solution.py:12
  133.1 111.6 %collective-permute-start.2 = (bf16[8,128,128]{2,1,0:T(8,128)(2,1)S(1)}, bf16[8,128,128]{2,1,0:T(8,128)(2,1)}, u32[]{:S(2)}, u32[]{:S(2)}) collective-permute-start(bf16[8,128,128]{2,1,0:T(8,128)(2,1)S(1)} %copy-done.4), channel_id=1, source_target_pairs={{0,192},{64,128},{128,64},{192,0},{256,448},{320,384},{384,320},{4... | collective-permute-start | bytes 786440 | tf_op jit(solution)/shard_map/ppermute | solution.py:12
Sparse Core Ops, SparseCore 0:
  72.9 169.3 all-gather.2
where the time goes:
time: 254 us
  waiting for transfers between devices  149 us (59%)
  starting transfers between devices  74.7 us (29%)
  between operations  14.3 us (6%)
  matrix products  8.17 us (3%)
  local copies, waits for them, and re-layouts  4.54 us (2%)
  other arithmetic  2.7 us (1%)
    all_gather x1, waiting for transfers between devices, on_device(): lax.all_gather(head, 'sub', axis=0, tiled=True)  76.8 us
    ppermute x8, waiting for transfers between devices, from_partner(): return lax.ppermute(value, axis, pairs)  46.7 us
    ppermute x8, starting transfers between devices, from_partner(): return lax.ppermute(value, axis, pairs)  38.1 us
    all_to_all x1, starting transfers between devices, on_device(): lax.all_to_all(partial.reshape(n_sub, width // n_sub, width), 'sub', 0, 0...  36.6 us
    all_to_all x1, waiting for transfers between devices, on_device(): lax.all_to_all(partial.reshape(n_sub, width // n_sub, width), 'sub', 0, 0...  25.7 us
  transfers between devices with their start and end apart: 10, of which 5 were waited for; matrix products, arithmetic and copies ran while one was open for 2% of the time, Pallas kernels for 0%

commit v1 on v0

--- a/solution.py
+++ b/solution.py
@@ -51,7 +51,9 @@
     quarter = width // merged
     column = group_index % merged * quarter
     head = lax.dynamic_slice_in_dim(panel[:block_size], column, quarter, 1)
-    piece = lax.all_gather(head, "sub", axis=0, tiled=True).reshape(n_sub, block_size, quarter)
+    piece = jnp.concatenate(
+        lax.all_to_all(jnp.stack([head] * lax.axis_size("sub")), "sub", 0, 0), axis=0
+    ).reshape(n_sub, block_size, quarter)
     picked = jnp.take(piece, rows_all, axis=0)
     parent_out = jnp.einsum(
         "kab,kbm->am", vals_all, picked, preferred_element_type=jnp.float32

time: 254 us -> 218 us (0.86)
  waiting for transfers between devices: 149 us -> 121 us
  between operations: 14.3 us -> 0.89 us
  starting transfers between devices: 74.7 us -> 79.6 us
    all_gather x1 -> x0, waiting for transfers between devices: 76.8 us -> none  [on_device(): lax.all_gather(head, 'sub', axis=0, tiled=True)]
    ppermute x8, waiting for transfers between devices: 46.7 us -> 77.4 us  [from_partner(): return lax.ppermute(value, axis, pairs)]
    all_to_all x0 -> x1, waiting for transfers between devices: none -> 15.5 us  [on_device(): lax.all_to_all(jnp.stack([head] * lax.axis_size('sub')), 'sub', 0, 0)]
    all_to_all x0 -> x1, starting transfers between devices: none -> 6.18 us  [on_device(): lax.all_to_all(jnp.stack([head] * lax.axis_size('sub')), 'sub', 0, 0)]
where the time goes in v1:
time: 218 us; the launch traced here: 216 us
  waiting for transfers between devices  121 us (56%)
  starting transfers between devices  79.6 us (37%)
  matrix products  6.97 us (3%)
  local copies, waits for them, and re-layouts  6.73 us (3%)
    ppermute x8, waiting for transfers between devices, from_partner(): return lax.ppermute(value, axis, pairs)  77.4 us
    ppermute x8, starting transfers between devices, from_partner(): return lax.ppermute(value, axis, pairs)  37 us
    all_to_all x1, starting transfers between devices, on_device(): lax.all_to_all(partial.reshape(n_sub, width // n_sub, width), 'sub', 0, 0...  36.5 us
    all_to_all x1, waiting for transfers between devices, on_device(): lax.all_to_all(partial.reshape(n_sub, width // n_sub, width), 'sub', 0, 0...  27.7 us
    all_to_all x1, waiting for transfers between devices, on_device(): lax.all_to_all(jnp.stack([head] * lax.axis_size('sub')), 'sub', 0, 0)  15.5 us
    all_to_all x1, starting transfers between devices, on_device(): lax.all_to_all(jnp.stack([head] * lax.axis_size('sub')), 'sub', 0, 0)  6.18 us
  transfers between devices with their start and end apart: 10, of which 5 were waited for; matrix products, arithmetic and copies ran while one was open for 2% of the time, Pallas kernels for 0%

profile of v1, /device:TPU:1, one launch (start us, length us, event | category | flops | bytes accessed | tf_op | source)
XLA Modules:
  0.0 216.4 jit_solution(8641482025308574498)
XLA Ops:
  0.6 0.8 eq.17
  2.1 1.0 fusion.5
  3.3 1.2 fusion.8
  4.5 8.4 %collective-permute-start.6 = (bf16[1024,512]{1,0:T(8,128)(2,1)S(1)}, bf16[1024,512]{1,0:T(8,128)(2,1)S(1)}, u32[]{:S(2)}, u32[]{:S(2)}) collective-permute-start(bf16[1024,512]{1,0:T(8,128)(2,1)S(1)} %fusion.8), channel_id=1, source_target_pairs={{0,64},{64,0},{128,192},{192,128},{256,320},{320,256},{384,448},{4... | collective-permute-start | bytes 3145736 | tf_op jit(solution)/shard_map/ppermute | solution.py:12
  13.0 33.9 %collective-permute-done.6 = bf16[1024,512]{1,0:T(8,128)(2,1)S(1)} collective-permute-done((bf16[1024,512]{1,0:T(8,128)(2,1)S(1)}, bf16[1024,512]{1,0:T(8,128)(2,1)S(1)}, u32[]{:S(2)}, u32[]{:S(2)}) %collective-permute-start.6) | collective-permute-done | bytes 1048608 | tf_op jit(solution)/shard_map/ppermute | solution.py:12
  47.6 3.8 %collective-permute-start.7 = (bf16[1024,512]{1,0:T(8,128)(2,1)S(1)}, bf16[1024,512]{1,0:T(8,128)(2,1)S(1)}, u32[]{:S(2)}, u32[]{:S(2)}) collective-permute-start(bf16[1024,512]{1,0:T(8,128)(2,1)S(1)} %bitcast.53), channel_id=1, source_target_pairs={{0,128},{64,192},{128,0},{192,64},{256,384},{320,448},{384,256},{4... | collective-permute-start | bytes 3145736 | tf_op jit(solution)/shard_map/ppermute | solution.py:12
  51.4 12.2 %collective-permute-done.7 = bf16[1024,512]{1,0:T(8,128)(2,1)S(1)} collective-permute-done((bf16[1024,512]{1,0:T(8,128)(2,1)S(1)}, bf16[1024,512]{1,0:T(8,128)(2,1)S(1)}, u32[]{:S(2)}, u32[]{:S(2)}) %collective-permute-start.7) | collective-permute-done | bytes 1048608 | tf_op jit(solution)/shard_map/ppermute | solution.py:12
  64.4 1.8 convolution_bitcast_fusion
  66.2 36.5 %all-to-all-start.1 = ((f32[64,8,512]{2,1,0:T(8,128)}), f32[64,8,512]{2,1,0:T(8,128)S(1)}, u32[]{:S(2)}, u32[]{:S(2)}) async-start(f32[64,8,512]{2,1,0:T(8,128)} %convolution_bitcast_fusion), calls=%async_computation.1 | async-start | bytes 2097152 | tf_op jit(solution)/shard_map/all_to_all | solution.py:64
  102.7 0.9 slice.15
  103.6 27.7 %all-to-all-done.1 = f32[64,8,512]{2,1,0:T(8,128)S(1)} async-done(((f32[64,8,512]{2,1,0:T(8,128)}), f32[64,8,512]{2,1,0:T(8,128)S(1)}, u32[]{:S(2)}, u32[]{:S(2)}) %all-to-all-start.1) | async-done | bytes 1048608 | tf_op jit(solution)/shard_map/all_to_all | solution.py:64
  131.3 1.8 stack.2
  133.1 6.2 %all-to-all-start = ((bf16[64,128,128]{2,1,0:T(8,128)(2,1)}), bf16[64,128,128]{2,1,0:T(8,128)(2,1)}, u32[]{:S(2)}, u32[]{:S(2)}) async-start(bf16[64,128,128]{2,1,0:T(8,128)(2,1)} %stack.2), calls=%async_computation | async-start | bytes 4194304 | tf_op jit(solution)/shard_map/all_to_all | solution.py:55
  139.3 6.0 %collective-permute-start.5 = (s32[8]{0:T(128)S(1)}, s32[8]{0:T(128)S(1)}, u32[]{:S(2)}, u32[]{:S(2)}) collective-permute-start(s32[8]{0:T(128)S(1)} %copy-done.3), channel_id=1, source_target_pairs={{0,192},{64,128},{128,64},{192,0},{256,448},{320,384},{384,320},{4... | collective-permute-start | bytes 104 | tf_op jit(solution)/shard_map/ppermute | solution.py:12
  145.3 2.1 collective-permute-start.4
  147.5 4.1 %collective-permute-start.3 = (s32[8]{0:T(128)S(1)}, s32[8]{0:T(128)S(1)}, u32[]{:S(2)}, u32[]{:S(2)}) collective-permute-start(s32[8]{0:T(128)S(1)} %copy-done.3), channel_id=1, source_target_pairs={{0,64},{64,0},{128,192},{192,128},{256,320},{320,256},{384,448},{4... | collective-permute-start | bytes 104 | tf_op jit(solution)/shard_map/ppermute | solution.py:12
  151.6 3.1 %collective-permute-start.1 = (bf16[8,128,128]{2,1,0:T(8,128)(2,1)S(1)}, bf16[8,128,128]{2,1,0:T(8,128)(2,1)S(1)}, u32[]{:S(2)}, u32[]{:S(2)}) collective-permute-start(bf16[8,128,128]{2,1,0:T(8,128)(2,1)S(1)} %copy-done.6), channel_id=1, source_target_pairs={{0,128},{64,192},{128,0},{192,64},{256,384},{320,448},{384,256},{4... | collective-permute-start | bytes 786440 | tf_op jit(solution)/shard_map/ppermute | solution.py:12
  154.8 5.1 %collective-permute-start = (bf16[8,128,128]{2,1,0:T(8,128)(2,1)S(1)}, bf16[8,128,128]{2,1,0:T(8,128)(2,1)S(1)}, u32[]{:S(2)}, u32[]{:S(2)}) collective-permute-start(bf16[8,128,128]{2,1,0:T(8,128)(2,1)S(1)} %copy-done.6), channel_id=1, source_target_pairs={{0,64},{64,0},{128,192},{192,128},{256,320},{320,256},{384,448},{4... | collective-permute-start | bytes 786440 | tf_op jit(solution)/shard_map/ppermute | solution.py:12
  159.8 31.3 %collective-permute-done.5 = s32[8]{0:T(128)S(1)} collective-permute-done((s32[8]{0:T(128)S(1)}, s32[8]{0:T(128)S(1)}, u32[]{:S(2)}, u32[]{:S(2)}) %collective-permute-start.5) | collective-permute-done | bytes 64 | tf_op jit(solution)/shard_map/ppermute | solution.py:12
  191.2 4.3 %collective-permute-start.2 = (bf16[8,128,128]{2,1,0:T(8,128)(2,1)S(1)}, bf16[8,128,128]{2,1,0:T(8,128)(2,1)}, u32[]{:S(2)}, u32[]{:S(2)}) collective-permute-start(bf16[8,128,128]{2,1,0:T(8,128)(2,1)S(1)} %copy-done.6), channel_id=1, source_target_pairs={{0,192},{64,128},{128,64},{192,0},{256,448},{320,384},{384,320},{4... | collective-permute-start | bytes 786440 | tf_op jit(solution)/shard_map/ppermute | solution.py:12
  195.7 0.7 reduce_sum.9
  196.4 15.5 %all-to-all-done = bf16[64,128,128]{2,1,0:T(8,128)(2,1)} async-done(((bf16[64,128,128]{2,1,0:T(8,128)(2,1)}), bf16[64,128,128]{2,1,0:T(8,128)(2,1)}, u32[]{:S(2)}, u32[]{:S(2)}) %all-to-all-start) | async-done | bytes 2097184 | tf_op jit(solution)/shard_map/all_to_all | solution.py:55
  211.9 2.3 %gather_fusion = bf16[32,128,128]{2,1,0:T(8,128)(2,1)S(1)} fusion(bf16[64,128,128]{2,1,0:T(8,128)(2,1)} %all-to-all-done, s32[1024]{0:T(1024)S(1)} %pad_clamp_fusion), kind=kCustom, calls=%fused_computation | custom fusion | bytes 2097280 | tf_op jit(solution)/shard_map/jit(_take)/gather | solution.py:57
  214.3 2.1 fusion.11
  (27 shorter events, 2.5 us)
Async XLA Ops:
  0.6 1.4 copy-start
  2.1 1.2 copy-start.4
  4.5 42.6 %copy-start.2 = (bf16[2,128,128]{2,1,0:T(8,128)(2,1)S(1)}, bf16[2,128,128]{2,1,0:T(8,128)(2,1)}, u32[]{:S(2)}) copy-start(bf16[2,128,128]{2,1,0:T(8,128)(2,1)} %param.10) | copy-start | bytes 196612
  4.5 42.3 %collective-permute-start.6 = (bf16[1024,512]{1,0:T(8,128)(2,1)S(1)}, bf16[1024,512]{1,0:T(8,128)(2,1)S(1)}, u32[]{:S(2)}, u32[]{:S(2)}) collective-permute-start(bf16[1024,512]{1,0:T(8,128)(2,1)S(1)} %fusion.8), channel_id=1, source_target_pairs={{0,64},{64,0},{128,192},{192,128},{256,320},{320,256},{384,448},{4... | collective-permute-start | bytes 3145736 | tf_op jit(solution)/shard_map/ppermute | solution.py:12
  47.6 16.8 %copy-start.5 = (bf16[1024,512]{1,0:T(8,128)(2,1)S(1)}, bf16[1024,512]{1,0:T(8,128)(2,1)}, u32[]{:S(2)}) copy-start(bf16[1024,512]{1,0:T(8,128)(2,1)} %param.11) | copy-start | bytes 3145732
  47.6 16.0 %collective-permute-start.7 = (bf16[1024,512]{1,0:T(8,128)(2,1)S(1)}, bf16[1024,512]{1,0:T(8,128)(2,1)S(1)}, u32[]{:S(2)}, u32[]{:S(2)}) collective-permute-start(bf16[1024,512]{1,0:T(8,128)(2,1)S(1)} %bitcast.53), channel_id=1, source_target_pairs={{0,128},{64,192},{128,0},{192,64},{256,384},{320,448},{384,256},{4... | collective-permute-start | bytes 3145736 | tf_op jit(solution)/shard_map/ppermute | solution.py:12
  64.4 1.8 copy-start.1
  66.2 65.1 %all-to-all-start.1 = ((f32[64,8,512]{2,1,0:T(8,128)}), f32[64,8,512]{2,1,0:T(8,128)S(1)}, u32[]{:S(2)}, u32[]{:S(2)}) async-start(f32[64,8,512]{2,1,0:T(8,128)} %convolution_bitcast_fusion), calls=%async_computation.1 | async-start | bytes 2097152 | tf_op jit(solution)/shard_map/all_to_all | solution.py:64
  133.1 6.2 %copy-start.3 = (s32[8]{0:T(128)S(1)}, s32[8]{0:T(128)}, u32[]{:S(2)}) copy-start(s32[8]{0:T(128)} %param.13) | copy-start | bytes 100
  133.1 18.5 %copy-start.6 = (bf16[8,128,128]{2,1,0:T(8,128)(2,1)S(1)}, bf16[8,128,128]{2,1,0:T(8,128)(2,1)}, u32[]{:S(2)}) copy-start(bf16[8,128,128]{2,1,0:T(8,128)(2,1)} %param.12) | copy-start | bytes 786436
  133.1 78.8 %all-to-all-start = ((bf16[64,128,128]{2,1,0:T(8,128)(2,1)}), bf16[64,128,128]{2,1,0:T(8,128)(2,1)}, u32[]{:S(2)}, u32[]{:S(2)}) async-start(bf16[64,128,128]{2,1,0:T(8,128)(2,1)} %stack.2), calls=%async_computation | async-start | bytes 4194304 | tf_op jit(solution)/shard_map/all_to_all | solution.py:55
  139.3 51.8 %collective-permute-start.5 = (s32[8]{0:T(128)S(1)}, s32[8]{0:T(128)S(1)}, u32[]{:S(2)}, u32[]{:S(2)}) collective-permute-start(s32[8]{0:T(128)S(1)} %copy-done.3), channel_id=1, source_target_pairs={{0,192},{64,128},{128,64},{192,0},{256,448},{320,384},{384,320},{4... | collective-permute-start | bytes 104 | tf_op jit(solution)/shard_map/ppermute | solution.py:12
  145.3 50.2 %collective-permute-start.4 = (s32[8]{0:T(128)S(1)}, s32[8]{0:T(128)S(1)}, u32[]{:S(2)}, u32[]{:S(2)}) collective-permute-start(s32[8]{0:T(128)S(1)} %copy-done.3), channel_id=1, source_target_pairs={{0,128},{64,192},{128,0},{192,64},{256,384},{320,448},{384,256},{4... | collective-permute-start | bytes 104 | tf_op jit(solution)/shard_map/ppermute | solution.py:12
  147.5 48.1 %collective-permute-start.3 = (s32[8]{0:T(128)S(1)}, s32[8]{0:T(128)S(1)}, u32[]{:S(2)}, u32[]{:S(2)}) collective-permute-start(s32[8]{0:T(128)S(1)} %copy-done.3), channel_id=1, source_target_pairs={{0,64},{64,0},{128,192},{192,128},{256,320},{320,256},{384,448},{4... | collective-permute-start | bytes 104 | tf_op jit(solution)/shard_map/ppermute | solution.py:12
  151.6 62.7 %collective-permute-start.1 = (bf16[8,128,128]{2,1,0:T(8,128)(2,1)S(1)}, bf16[8,128,128]{2,1,0:T(8,128)(2,1)S(1)}, u32[]{:S(2)}, u32[]{:S(2)}) collective-permute-start(bf16[8,128,128]{2,1,0:T(8,128)(2,1)S(1)} %copy-done.6), channel_id=1, source_target_pairs={{0,128},{64,192},{128,0},{192,64},{256,384},{320,448},{384,256},{4... | collective-permute-start | bytes 786440 | tf_op jit(solution)/shard_map/ppermute | solution.py:12
  154.8 59.5 %collective-permute-start = (bf16[8,128,128]{2,1,0:T(8,128)(2,1)S(1)}, bf16[8,128,128]{2,1,0:T(8,128)(2,1)S(1)}, u32[]{:S(2)}, u32[]{:S(2)}) collective-permute-start(bf16[8,128,128]{2,1,0:T(8,128)(2,1)S(1)} %copy-done.6), channel_id=1, source_target_pairs={{0,64},{64,0},{128,192},{192,128},{256,320},{320,256},{384,448},{4... | collective-permute-start | bytes 786440 | tf_op jit(solution)/shard_map/ppermute | solution.py:12
  191.2 23.1 %collective-permute-start.2 = (bf16[8,128,128]{2,1,0:T(8,128)(2,1)S(1)}, bf16[8,128,128]{2,1,0:T(8,128)(2,1)}, u32[]{:S(2)}, u32[]{:S(2)}) collective-permute-start(bf16[8,128,128]{2,1,0:T(8,128)(2,1)S(1)} %copy-done.6), channel_id=1, source_target_pairs={{0,192},{64,128},{128,64},{192,0},{256,448},{320,384},{384,320},{4... | collective-permute-start | bytes 786440 | tf_op jit(solution)/shard_map/ppermute | solution.py:12
